TPU v7x, 32 devices: a whole 2x2x4 slice. The times are simulated.
32 devices in a mesh: section: 4 (over y, core), seq: 8 (over z, x).
Axes of the slice: x: 2, y: 2, z: 4, core: 2. Of those that a mesh axis runs over, the one named last changes fastest.
Arguments:
- queries: bfloat16 [4, 2048, 4096], P('section', 'seq'), may hold values from -42 to 42
- keys: bfloat16 [4, 2048, 512], P('section', 'seq'), may hold values from -6 to 6
- values: bfloat16 [4, 2048, 512], P('section', 'seq'), may hold values from -6 to 6
- out_grads: bfloat16 [4, 2048, 4096], P('section', 'seq'), may hold values from -6 to 6
- random_blocks: int32 [4, 32, 3], P('section'), may hold values from 0 to 31, as said below
- global_blocks: int32 [4, 2], P('section'), may hold values from 0 to 31, as said below
- pad_lengths: int32 [4, 8], P('section'), may hold values from 0 to 63, as said below
Outputs:
- passed_query_grad: bfloat16 [4, 2048, 4096], P('section', 'seq')
- passed_key_grad: bfloat16 [4, 2048, 512], P('section', 'seq')
- passed_value_grad: bfloat16 [4, 2048, 512], P('section', 'seq')
Inputs may be any that keep to these rules, and one draw needn't show every extreme that they name: `random_blocks`: over the 12 random blocks named by one shard's query blocks, the blocks of any one shard are named at most 2 times, and on every shard some shard's blocks exactly 2 times; within one random slot (one column) at most 1 times, and exactly 1 times for some shard. `global_blocks`: the 2 global blocks of a section are distinct. `pad_lengths`: every section has a shard with exactly 63 padding tokens.
All inputs are finite; a program needn't handle non-finite values.
Results may differ from a plain program's by a relative error of at most 0.007.
Values may be sent and summed in bfloat16 or wider, within the bound.
No kernel may reach another device: no remote copies, remote signals or barrier semaphores. Data moves between devices by JAX's collectives and lax.ppermute only.
A program may use at most 128 MiB of HBM per device.

v0:
```python
import math
import jax
import jax.numpy as jnp
from jax import lax
from jax.sharding import PartitionSpec as P

HDIM = 128
BLK = 64
GLOB = 2
RAND = 3


def extended_2(array, sides, width):
    for axis, dim in sides:
        devices, length = (lax.axis_size(axis), array.shape[dim])
        up = [(i, (i + 1) % devices) for i in range(devices - 1)]
        down = [(j, i) for i, j in up]
        last = lax.slice_in_dim(array, length - width, length, axis=dim)
        leading = lax.slice_in_dim(array, 0, width, axis=dim)
        before = lax.ppermute(last, axis, up)
        after = lax.ppermute(leading, axis, down)
        array = jnp.concatenate([before, array, after], axis=dim)
    return array


def broadcast(array, axis, root):
    mine = lax.axis_index(axis) == root
    return lax.psum(jnp.where(mine, array, jnp.zeros_like(array)), axis)


def from_behind(block, axis, distance):
    devices = range(lax.axis_size(axis))
    route = [((i - distance) % len(devices), i) for i in devices]
    return lax.ppermute(block, axis, route)


def block_backward(query_rows, grad_rows, key_tiles, value_tiles, key_live):
    nblocks, block_len, qwidth = query_rows.shape
    ntiles = key_tiles.shape[1]
    kwidth = key_tiles.shape[-1]
    heads_kv = kwidth // HDIM
    group = qwidth // kwidth
    score_scale = 1.0 / math.sqrt(HDIM)
    query_heads = jnp.moveaxis(query_rows.reshape(nblocks, block_len, heads_kv, group, HDIM), 2, 0)
    grad_heads = jnp.moveaxis(grad_rows.reshape(nblocks, block_len, heads_kv, group, HDIM), 2, 0)
    key_heads = jnp.moveaxis(key_tiles.reshape(nblocks, ntiles, block_len, heads_kv, HDIM), 3, 0)
    value_heads = jnp.moveaxis(
        value_tiles.reshape(nblocks, ntiles, block_len, heads_kv, HDIM), 3, 0
    )
    live_mask = key_live[:, None, None, :, :]

    def one_head(inputs):
        query_one, grad_one, key_one, value_one = inputs
        scores = (
            jnp.einsum("bqgd,btkd->bgqtk", query_one, key_one, preferred_element_type=jnp.float32)
            * score_scale
        )
        scores = jnp.where(live_mask, scores, -1e30)
        row_max = jnp.max(scores, axis=(3, 4), keepdims=True)
        log_total = row_max + jnp.log(
            jnp.sum(jnp.exp(scores - row_max), axis=(3, 4), keepdims=True)
        )
        probs = jnp.exp(scores - log_total)
        probs_low = probs.astype(jnp.bfloat16)
        output = jnp.einsum(
            "bgqtk,btkd->bqgd", probs_low, value_one, preferred_element_type=jnp.float32
        )
        row_dot = jnp.sum(grad_one * output, axis=-1)
        prob_grad = jnp.einsum(
            "bqgd,btkd->bgqtk", grad_one, value_one, preferred_element_type=jnp.float32
        )
        score_grad = (
            probs * (prob_grad - jnp.transpose(row_dot, (0, 2, 1))[:, :, :, None, None])
        ).astype(jnp.bfloat16)
        query_grad = (
            jnp.einsum("bgqtk,btkd->bqgd", score_grad, key_one, preferred_element_type=jnp.float32)
            * score_scale
        )
        key_grad = (
            jnp.einsum(
                "bgqtk,bqgd->btkd", score_grad, query_one, preferred_element_type=jnp.float32
            )
            * score_scale
        )
        value_grad = jnp.einsum(
            "bgqtk,bqgd->btkd", probs_low, grad_one, preferred_element_type=jnp.float32
        )
        return (query_grad, key_grad, value_grad)

    query_grad, key_grad, value_grad = lax.map(
        one_head, (query_heads, grad_heads, key_heads, value_heads)
    )
    return (
        jnp.moveaxis(query_grad, 0, 2).reshape(nblocks, block_len, qwidth),
        jnp.moveaxis(key_grad, 0, 3).reshape(nblocks, ntiles, block_len, kwidth),
        jnp.moveaxis(value_grad, 0, 3).reshape(nblocks, ntiles, block_len, kwidth),
    )


def request_plan(request_lists, this_shard, query_blocks):
    shards, count = request_lists.shape
    capacity = -(-count // shards)
    owner_ids = request_lists // query_blocks
    local_ids = request_lists % query_blocks
    order = jnp.arange(count, dtype=jnp.int32)
    earlier = order[None, :] < order[:, None]
    same_owner = owner_ids[:, :, None] == owner_ids[:, None, :]
    slot_rank = jnp.sum(same_owner & earlier[None], axis=2)
    slot_ids = jnp.arange(capacity, dtype=jnp.int32)
    chosen = (owner_ids[:, None, :] == this_shard) & (
        slot_rank[:, None, :] == slot_ids[None, :, None]
    )
    serve_block = jnp.sum(jnp.where(chosen, local_ids[:, None, :], 0), axis=2)
    slot_used = jnp.any(chosen, axis=2)
    owner_mine = lax.dynamic_index_in_dim(owner_ids, this_shard, 0, keepdims=False)
    rank_mine = lax.dynamic_index_in_dim(slot_rank, this_shard, 0, keepdims=False)
    return (serve_block, slot_used, owner_mine, rank_mine)


def serve_tiles(own_blocks, request_info):
    serve_block, slot_used = (request_info[0], request_info[1])
    shards, capacity = serve_block.shape
    gathered = jnp.take(own_blocks, serve_block.reshape(-1), axis=1)
    gathered = gathered.reshape(2, shards, capacity, own_blocks.shape[2], own_blocks.shape[3])
    return jnp.where(slot_used[None, :, :, None, None], gathered, jnp.zeros((), own_blocks.dtype))


def pick_tiles(received, request_info):
    return received[:, request_info[2], request_info[3]]


def place_terms(terms, request_info):
    serve_block = request_info[0]
    shards, capacity = serve_block.shape
    holder = jnp.zeros((2, shards, capacity, terms.shape[2], terms.shape[3]), terms.dtype)
    return holder.at[:, request_info[2], request_info[3]].set(terms)


def absorb_terms(received, request_info, query_blocks):
    serve_block, slot_used = (request_info[0], request_info[1])
    onehot = (
        slot_used[:, :, None]
        & (serve_block[:, :, None] == jnp.arange(query_blocks, dtype=jnp.int32)[None, None, :])
    ).astype(jnp.bfloat16)
    return jnp.einsum("ncq,xncsk->xqsk", onehot, received, preferred_element_type=jnp.float32)


def token_live(tile_ids, pad_sizes, query_blocks, shard_tokens, total_blocks):
    valid = (tile_ids >= 0) & (tile_ids < total_blocks)
    safe_ids = jnp.clip(tile_ids, 0, total_blocks - 1)
    owner_shard = safe_ids // query_blocks
    shards = pad_sizes.shape[0]
    pad_of = jnp.sum(
        jnp.where(owner_shard[..., None] == jnp.arange(shards, dtype=jnp.int32), pad_sizes, 0),
        axis=-1,
    )
    within = (safe_ids % query_blocks)[..., None] * BLK + jnp.arange(BLK, dtype=jnp.int32)
    return valid[..., None] & (within < (shard_tokens - pad_of)[..., None])


def body(queries, keys, values, out_grads, random_blocks, global_blocks, pad_lengths):
    query_rows = queries[0]
    key_rows = keys[0]
    value_rows = values[0]
    grad_rows = out_grads[0]
    random_table = random_blocks[0]
    global_ids = global_blocks[0]
    pad_sizes = pad_lengths[0]
    shards = lax.axis_size("seq")
    this_shard = lax.axis_index("seq")
    shard_tokens, qwidth = query_rows.shape
    kwidth = key_rows.shape[1]
    query_blocks = shard_tokens // BLK
    total_blocks = query_blocks * shards
    near = 3 + GLOB
    kvpair = jnp.stack([key_rows, value_rows])
    extended = extended_2(kvpair, (("seq", 1),), BLK)
    ext_blocks = extended.reshape(2, query_blocks + 2, BLK, kwidth)
    window = jnp.stack(
        [ext_blocks[:, offset : offset + query_blocks] for offset in range(3)], axis=2
    )
    own_blocks = kvpair.reshape(2, query_blocks, BLK, kwidth)
    global_list = []
    for glob_num in range(GLOB):
        owner_dev = global_ids[glob_num] // query_blocks
        local_tile = lax.dynamic_index_in_dim(
            own_blocks, global_ids[glob_num] % query_blocks, 1, keepdims=False
        )
        global_list.append(broadcast(local_tile, "seq", owner_dev))
    global_tiles = jnp.stack(global_list, axis=1)
    random_three = random_table.reshape(shards, query_blocks, RAND)
    slot_plans = []
    pieces = []
    for slot_num in range(RAND):
        slot_plan = request_plan(random_three[:, :, slot_num], this_shard, query_blocks)
        received = lax.all_to_all(
            serve_tiles(own_blocks, slot_plan), "seq", split_axis=1, concat_axis=1, tiled=True
        )
        pieces.append(pick_tiles(received, slot_plan))
        slot_plans.append(slot_plan)
    fetched = jnp.stack(pieces, axis=2)
    spread_global = jnp.broadcast_to(global_tiles[:, None], (2, query_blocks, GLOB, BLK, kwidth))
    all_tiles = jnp.concatenate([window, spread_global, fetched], axis=2)
    base_ids = this_shard * query_blocks + jnp.arange(query_blocks, dtype=jnp.int32)
    window_ids = base_ids[:, None] + jnp.arange(-1, 2, dtype=jnp.int32)[None, :]
    my_random = lax.dynamic_index_in_dim(random_three, this_shard, 0, keepdims=False)
    tile_ids = jnp.concatenate(
        [window_ids, jnp.broadcast_to(global_ids[None, :], (query_blocks, GLOB)), my_random], axis=1
    )
    key_live = token_live(tile_ids, pad_sizes, query_blocks, shard_tokens, total_blocks)
    query_grad, key_terms, value_terms = block_backward(
        query_rows.reshape(query_blocks, BLK, qwidth),
        grad_rows.reshape(query_blocks, BLK, qwidth),
        all_tiles[0],
        all_tiles[1],
        key_live,
    )
    contrib = jnp.stack([key_terms, value_terms])
    local_sum = contrib[:, :, 1]
    local_sum = local_sum + jnp.pad(contrib[:, 1:, 0], ((0, 0), (0, 1), (0, 0), (0, 0)))
    local_sum = local_sum + jnp.pad(contrib[:, :-1, 2], ((0, 0), (1, 0), (0, 0), (0, 0)))
    edge_out = jnp.concatenate([contrib[:, 0, 0], contrib[:, query_blocks - 1, 2]], axis=1)
    edge_in = extended_2(edge_out.astype(jnp.bfloat16), (("seq", 1),), BLK).astype(edge_out.dtype)
    local_sum = local_sum.at[:, 0].add(edge_in[:, :BLK])
    local_sum = local_sum.at[:, query_blocks - 1].add(edge_in[:, 3 * BLK :])
    global_part = jnp.sum(contrib[:, :, 3:near], axis=1)
    global_total = lax.psum(global_part, "seq")
    global_pick = (
        (global_ids[:, None] // query_blocks == this_shard)
        & (global_ids[:, None] % query_blocks == jnp.arange(query_blocks, dtype=jnp.int32)[None, :])
    ).astype(jnp.float32)
    local_sum = local_sum + jnp.einsum(
        "gq,xgsk->xqsk", global_pick, global_total, precision=lax.Precision.HIGHEST
    )
    random_terms = contrib[:, :, near:].astype(jnp.bfloat16)
    for slot_num in range(RAND):
        returned = lax.all_to_all(
            place_terms(random_terms[:, :, slot_num], slot_plans[slot_num]),
            "seq",
            split_axis=1,
            concat_axis=1,
            tiled=True,
        )
        local_sum = local_sum + absorb_terms(returned, slot_plans[slot_num], query_blocks)
    key_grad = local_sum[0].reshape(shard_tokens, kwidth).astype(jnp.bfloat16)
    value_grad = local_sum[1].reshape(shard_tokens, kwidth).astype(jnp.bfloat16)
    query_low = query_grad.reshape(shard_tokens, qwidth).astype(jnp.bfloat16)
    packed = jnp.concatenate([query_low, key_grad, value_grad], axis=-1)
    handed = from_behind(packed, "section", -1)
    return (
        handed[None, :, :qwidth],
        handed[None, :, qwidth : qwidth + kwidth],
        handed[None, :, qwidth + kwidth :],
    )


def solution(mesh):
    in_specs = (
        P("section", "seq", None),
        P("section", "seq", None),
        P("section", "seq", None),
        P("section", "seq", None),
        P("section", None, None),
        P("section", None),
        P("section", None),
    )
    out_specs = (P("section", "seq", None), P("section", "seq", None), P("section", "seq", None))
    return jax.shard_map(body, mesh=mesh, in_specs=in_specs, out_specs=out_specs, check_vma=False)
```

profile of v0, /device:TPU:1, one launch (start us, length us, event | category | flops | bytes accessed | tf_op | source)
XLA Modules:
  0.0 463.5 jit_solution(16679181156214838141)
XLA Ops:
  9.2 4.0 collective-permute-start
  17.7 6.4 %all-to-all-start = ((bf16[2,8,1,64,512]{4,3,0,2,1:T(8,128)(2,1)}), bf16[2,8,1,64,512]{4,3,0,2,1:T(8,128)(2,1)S(1)}, u32[]{:S(2)}, u32[]{:S(2)}) async-start(bf16[2,8,1,64,512]{4,3,0,2,1:T(8,128)(2,1)} %fusion.54), calls=%async_computation | async-start | bytes 2097152 | tf_op jit(solution)/shard_map/all_to_all | solution.py:196
  35.6 15.4 %all-to-all-done = bf16[2,8,1,64,512]{4,3,0,2,1:T(8,128)(2,1)S(1)} async-done(((bf16[2,8,1,64,512]{4,3,0,2,1:T(8,128)(2,1)}), bf16[2,8,1,64,512]{4,3,0,2,1:T(8,128)(2,1)S(1)}, u32[]{:S(2)}, u32[]{:S(2)}) %all-to-all-start) | async-done | bytes 1048608 | tf_op jit(solution)/shard_map/all_to_all | solution.py:196
  51.1 5.3 %all-to-all-start.1 = ((bf16[2,8,1,64,512]{4,3,0,2,1:T(8,128)(2,1)}), bf16[2,8,1,64,512]{4,3,0,2,1:T(8,128)(2,1)S(1)}, u32[]{:S(2)}, u32[]{:S(2)}) async-start(bf16[2,8,1,64,512]{4,3,0,2,1:T(8,128)(2,1)} %fusion.53), calls=%async_computation.1 | async-start | bytes 2097152 | tf_op jit(solution)/shard_map/all_to_all | solution.py:196
  57.9 2.4 fusion.52
  60.3 21.6 %all-to-all-done.1 = bf16[2,8,1,64,512]{4,3,0,2,1:T(8,128)(2,1)S(1)} async-done(((bf16[2,8,1,64,512]{4,3,0,2,1:T(8,128)(2,1)}), bf16[2,8,1,64,512]{4,3,0,2,1:T(8,128)(2,1)S(1)}, u32[]{:S(2)}, u32[]{:S(2)}) %all-to-all-start.1) | async-done | bytes 1048608 | tf_op jit(solution)/shard_map/all_to_all | solution.py:196
  82.0 4.8 %all-to-all-start.2 = ((bf16[2,8,1,64,512]{4,3,0,2,1:T(8,128)(2,1)}), bf16[2,8,1,64,512]{4,3,0,2,1:T(8,128)(2,1)}, u32[]{:S(2)}, u32[]{:S(2)}) async-start(bf16[2,8,1,64,512]{4,3,0,2,1:T(8,128)(2,1)} %fusion.52), calls=%async_computation.2 | async-start | bytes 2097152 | tf_op jit(solution)/shard_map/all_to_all | solution.py:196
  87.4 3.6 copy.201
  95.4 21.6 %all-reduce.8.cloned.1.call-done = (bf16[2,1,64,512]{3,2,1,0:T(8,128)(2,1)}, bf16[2,1,64,512]{3,2,1,0:T(8,128)(2,1)}) async-done(((bf16[2,1,64,512]{3,2,1,0:T(8,128)(2,1)}, bf16[2,1,64,512]{3,2,1,0:T(8,128)(2,1)}), (bf16[2,1,64,512]{3,2,1,0:T(8,128)(2,1)}, bf16[2,1,64,512]{3,2,1,0:T(8,128)(2,1)})) %all-reduce.8.cloned.1.call-update) | async-done | bytes 262160 | tf_op jit(solution)/shard_map/psum | solution.py:28
  127.2 4.0 fusion.130
  135.4 4.0 reshape_squeeze.13
  139.4 3.5 copy.160
  142.8 77.5 %while.17 = (s32[]{:T(128)}, bf16[4,4,64,8,128]{4,2,3,1,0:T(8,128)(2,1)}, f32[4,4,8,64,128]{4,3,2,1,0:T(8,128)}, f32[4,4,8,64,128]{4,3,2,1,0:T(8,128)}, bf16[4,4...) while((s32[]{:T(128)}, ...), condition=%wide.region_16.18_spmd.clone, body=%wide.region_12.17_spmd.clone.sunk | while | flops 1633945600 | bytes 56234432 | solution.py:90
  148.6 3.6 fusion.171
  152.2 2.9 fusion.167
  155.1 3.0 fusion.168
  168.0 3.5 fusion.171
  171.5 2.9 fusion.167
  174.4 3.0 fusion.168
  187.4 3.6 fusion.171
  190.9 2.9 fusion.167
  193.9 3.0 fusion.168
  206.7 3.6 fusion.171
  210.3 2.9 fusion.167
  213.2 3.0 fusion.168
  220.3 7.8 %copy.163 = f32[4,8,64,4,128]{4,3,2,0,1:T(4,128)} copy(f32[4,8,64,4,128]{4,2,1,0,3:T(8,128)} %bitcast.563) | data formatting | bytes 8388608 | tf_op jit(solution)/shard_map/transpose | solution.py:95
  228.1 5.5 %stack_reshape.6 = f32[1,4,8,64,512]{4,3,0,1,2:T(8,128)} reshape(f32[4,8,64,4,128]{4,3,2,0,1:T(4,128)} %copy.163) | data formatting | bytes 8388608 | tf_op jit(solution)/shard_map/stack;reshape | solution.py:218
  233.6 5.0 %constant_dynamic-update-slice_fusion.3 = f32[2,4,8,64,512]{4,3,0,1,2:T(8,128)} fusion(f32[1,4,8,64,512]{4,3,0,1,2:T(8,128)} %stack_reshape.6), kind=kLoop, calls=%fused_computation.124 | loop fusion | bytes 8388608
  238.6 5.6 %copy.164 = f32[4,8,64,4,128]{4,3,2,0,1:T(4,128)} copy(f32[4,8,64,4,128]{4,2,1,0,3:T(8,128)S(1)} %bitcast.564) | data formatting | bytes 8388608 | tf_op jit(solution)/shard_map/transpose | solution.py:96
  244.1 5.5 %stack_reshape.7 = f32[1,4,8,64,512]{4,3,0,1,2:T(8,128)} reshape(f32[4,8,64,4,128]{4,3,2,0,1:T(4,128)} %copy.164) | data formatting | bytes 8388608 | tf_op jit(solution)/shard_map/stack;reshape | solution.py:218
  249.6 4.8 %constant_dynamic-update-slice_fusion.2 = f32[2,4,8,64,512]{4,3,0,1,2:T(8,128)} fusion(f32[2,4,8,64,512]{4,3,0,1,2:T(8,128)} %constant_dynamic-update-slice_fusion.3, f32[1,4,8,64,512]{4,3,0,1,2:T(8,128)} %stack_reshape.7), kind=kLoop, calls=%fused_computation.123 | loop fusion | bytes 8388608 | tf_op jit(solution)/shard_map/stack | solution.py:218
  254.4 4.0 convert.13
  262.9 3.7 all-to-all-start.3
  268.6 22.3 %all-to-all-done.3 = bf16[2,8,1,64,512]{4,3,0,2,1:T(8,128)(2,1)S(1)} async-done(((bf16[2,8,1,64,512]{4,3,0,2,1:T(8,128)(2,1)}), bf16[2,8,1,64,512]{4,3,0,2,1:T(8,128)(2,1)S(1)}, u32[]{:S(2)}, u32[]{:S(2)}) %all-to-all-start.3) | async-done | bytes 1048608 | tf_op jit(solution)/shard_map/all_to_all | solution.py:237
  290.9 5.1 %all-to-all-start.4 = ((bf16[2,8,1,64,512]{4,3,0,2,1:T(8,128)(2,1)}), bf16[2,8,1,64,512]{4,3,0,2,1:T(8,128)(2,1)}, u32[]{:S(2)}, u32[]{:S(2)}) async-start(bf16[2,8,1,64,512]{4,3,0,2,1:T(8,128)(2,1)} %copy.173), calls=%async_computation.4 | async-start | bytes 2097152 | tf_op jit(solution)/shard_map/all_to_all | solution.py:237
  301.3 19.4 %all-to-all-done.4 = bf16[2,8,1,64,512]{4,3,0,2,1:T(8,128)(2,1)} async-done(((bf16[2,8,1,64,512]{4,3,0,2,1:T(8,128)(2,1)}), bf16[2,8,1,64,512]{4,3,0,2,1:T(8,128)(2,1)}, u32[]{:S(2)}, u32[]{:S(2)}) %all-to-all-start.4) | async-done | bytes 1048608 | tf_op jit(solution)/shard_map/all_to_all | solution.py:237
  320.6 5.1 %all-to-all-start.5 = ((bf16[2,8,1,64,512]{4,3,0,2,1:T(8,128)(2,1)}), bf16[2,8,1,64,512]{4,3,0,2,1:T(8,128)(2,1)}, u32[]{:S(2)}, u32[]{:S(2)}) async-start(bf16[2,8,1,64,512]{4,3,0,2,1:T(8,128)(2,1)} %copy.176), calls=%async_computation.5 | async-start | bytes 2097152 | tf_op jit(solution)/shard_map/all_to_all | solution.py:237
  327.9 3.7 collective-permute-start.2
  334.1 2.5 fusion.48
  336.6 4.3 copy.162
  340.9 2.8 convert_element_type.53
  346.5 2.9 copy.167
  350.6 6.1 %scatter-add.9 = f32[2,4,64,512]{3,1,2,0:T(4,128)} dynamic-update-slice(f32[2,4,64,512]{3,1,2,0:T(4,128)} %copy.167, f32[2,1,64,512]{3,1,2,0:T(1,128)S(1)} %copy_add_fusion, s32[]{:T(128)} %constant.241.clone.1, s32[]{:T(128)} %constant.245.clone.1, s32[]{:T(128)} %constant.241.clone.1, s32[]{:T(128)} %constant.241.clone.1) | dynamic-update-slice | bytes 524292 | tf_op jit(solution)/shard_map/scatter-add | solution.py:225
  356.8 54.0 %all-reduce.6.cloned.1.call-done = f32[2,2,64,512]{3,1,2,0:T(2,128)} async-done(((f32[2,2,64,512]{3,1,2,0:T(2,128)}), f32[2,2,64,512]{3,1,2,0:T(2,128)}) %all-reduce.6.cloned.1.call-update) | async-done | bytes 524304 | tf_op jit(solution)/shard_map/psum | solution.py:227
  410.8 2.6 fusion.45
  415.5 3.0 fusion.43
  421.4 2.5 collective-permute-start.4
  424.0 30.4 %collective-permute-done.4 = bf16[256,5120]{1,0:T(8,128)(2,1)S(1)} collective-permute-done((bf16[256,5120]{1,0:T(8,128)(2,1)S(1)}, bf16[256,5120]{1,0:T(8,128)(2,1)S(1)}, u32[]{:S(2)}, u32[]{:S(2)}) %collective-permute-start.4) | collective-permute-done | bytes 2621472 | tf_op jit(solution)/shard_map/ppermute | solution.py:34
  (198 shorter events, 100.1 us)
Async XLA Ops:
  7.2 17.0 %copy-start.20 = (s32[1,2]{1,0:T(1,128)S(1)}, s32[1,2]{1,0:T(1,128)}, u32[]{:S(2)}) copy-start(s32[1,2]{1,0:T(1,128)} %param.20) | copy-start | bytes 28
  9.2 83.6 %collective-permute-start = (bf16[2,64,512]{2,1,0:T(8,128)(2,1)S(1)}, bf16[2,64,512]{2,1,0:T(8,128)(2,1)S(1)}, u32[]{:S(2)}, u32[]{:S(2)}) collective-permute-start(bf16[2,64,512]{2,1,0:T(8,128)(2,1)S(1)} %get-tuple-element.194), channel_id=1, source_target_pairs={{0,1},{1,2},{2,3},{3,4},{4,5},{5,6},{6,7},{8,9},{9,10},{10,11},{11... | collective-permute-start | bytes 393224 | tf_op jit(solution)/shard_map/ppermute | solution.py:20
  13.1 79.7 %collective-permute-start.1 = (bf16[2,64,512]{2,1,0:T(8,128)(2,1)S(1)}, bf16[2,64,512]{2,1,0:T(8,128)(2,1)S(1)}, u32[]{:S(2)}, u32[]{:S(2)}) collective-permute-start(bf16[2,64,512]{2,1,0:T(8,128)(2,1)S(1)} %get-tuple-element.195), channel_id=1, source_target_pairs={{1,0},{2,1},{3,2},{4,3},{5,4},{6,5},{7,6},{9,8},{10,9},{11,10},{12... | collective-permute-start | bytes 393224 | tf_op jit(solution)/shard_map/ppermute | solution.py:21
  15.9 15.9 %copy-start.5 = (pred[8]{0:T(512)(128)(4,1)}, pred[8]{0:T(512)(128)(4,1)S(1)}, u32[]{:S(2)}) copy-start(pred[8]{0:T(512)(128)(4,1)S(1)} %get-tuple-element.173) | copy-start | bytes 28
  15.9 15.9 %copy-start.11 = (s32[8]{0:T(128)}, s32[8]{0:T(128)S(1)}, u32[]{:S(2)}) copy-start(s32[8]{0:T(128)S(1)} %fusion.79) | copy-start | bytes 100
  17.7 33.3 %all-to-all-start = ((bf16[2,8,1,64,512]{4,3,0,2,1:T(8,128)(2,1)}), bf16[2,8,1,64,512]{4,3,0,2,1:T(8,128)(2,1)S(1)}, u32[]{:S(2)}, u32[]{:S(2)}) async-start(bf16[2,8,1,64,512]{4,3,0,2,1:T(8,128)(2,1)} %fusion.54), calls=%async_computation | async-start | bytes 2097152 | tf_op jit(solution)/shard_map/all_to_all | solution.py:196
  24.1 92.9 %all-reduce.8.cloned.1.call-start = ((), (), s32[]{:S(2)}) async-start(), calls=%async_computation.7 | async-start | bytes 524288 | tf_op jit(solution)/shard_map/psum | solution.py:28
  30.8 20.3 %copy-start.7 = (pred[8]{0:T(512)(128)(4,1)}, pred[8]{0:T(512)(128)(4,1)S(1)}, u32[]{:S(2)}) copy-start(pred[8]{0:T(512)(128)(4,1)S(1)} %get-tuple-element.171) | copy-start | bytes 28
  30.8 20.2 %copy-start.13 = (s32[8]{0:T(128)}, s32[8]{0:T(128)S(1)}, u32[]{:S(2)}) copy-start(s32[8]{0:T(128)S(1)} %fusion.83) | copy-start | bytes 100
  31.8 24.8 %copy-start.22 = (s32[1,8]{1,0:T(1,128)S(1)}, s32[1,8]{1,0:T(1,128)}, u32[]{:S(2)}) copy-start(s32[1,8]{1,0:T(1,128)} %param.21) | copy-start | bytes 100
  32.6 27.7 %copy-start.9 = (pred[8]{0:T(512)(128)(4,1)}, pred[8]{0:T(512)(128)(4,1)S(1)}, u32[]{:S(2)}) copy-start(pred[8]{0:T(512)(128)(4,1)S(1)} %get-tuple-element.169) | copy-start | bytes 28
  32.7 27.7 %copy-start.15 = (s32[8]{0:T(128)}, s32[8]{0:T(128)S(1)}, u32[]{:S(2)}) copy-start(s32[8]{0:T(128)S(1)} %fusion.87) | copy-start | bytes 100
  51.1 30.9 %all-to-all-start.1 = ((bf16[2,8,1,64,512]{4,3,0,2,1:T(8,128)(2,1)}), bf16[2,8,1,64,512]{4,3,0,2,1:T(8,128)(2,1)S(1)}, u32[]{:S(2)}, u32[]{:S(2)}) async-start(bf16[2,8,1,64,512]{4,3,0,2,1:T(8,128)(2,1)} %fusion.53), calls=%async_computation.1 | async-start | bytes 2097152 | tf_op jit(solution)/shard_map/all_to_all | solution.py:196
  82.0 42.5 %all-to-all-start.2 = ((bf16[2,8,1,64,512]{4,3,0,2,1:T(8,128)(2,1)}), bf16[2,8,1,64,512]{4,3,0,2,1:T(8,128)(2,1)}, u32[]{:S(2)}, u32[]{:S(2)}) async-start(bf16[2,8,1,64,512]{4,3,0,2,1:T(8,128)(2,1)} %fusion.52), calls=%async_computation.2 | async-start | bytes 2097152 | tf_op jit(solution)/shard_map/all_to_all | solution.py:196
  87.4 3.6 copy-start.3
  148.6 3.6 copy-start.4
  168.0 3.6 copy-start.4
  187.3 3.6 copy-start.4
  206.7 3.6 copy-start.4
  233.6 5.0 %copy-start.1 = (f32[4,4,8,64,128]{4,3,2,1,0:T(8,128)S(1)}, f32[4,4,8,64,128]{4,3,2,1,0:T(8,128)}, u32[]{:S(2)}) copy-start(f32[4,4,8,64,128]{4,3,2,1,0:T(8,128)} %get-tuple-element.79) | copy-start | bytes 12582916
  258.4 2.0 copy-start
  260.4 0.6 copy-start.19
  260.5 6.2 %copy-start.18 = (s32[4]{0:T(128)S(1)}, s32[4]{0:T(128)}, u32[]{:S(2)}) copy-start(s32[4]{0:T(128)} %get-tuple-element.206) | copy-start | bytes 52
  262.9 33.1 %copy-start.21 = (s32[1,2]{1,0:T(1,128)S(1)}, s32[1,2]{1,0:T(1,128)}, u32[]{:S(2)}) copy-start(s32[1,2]{1,0:T(1,128)} %param.20) | copy-start | bytes 28
  262.9 28.0 %all-to-all-start.3 = ((bf16[2,8,1,64,512]{4,3,0,2,1:T(8,128)(2,1)}), bf16[2,8,1,64,512]{4,3,0,2,1:T(8,128)(2,1)S(1)}, u32[]{:S(2)}, u32[]{:S(2)}) async-start(bf16[2,8,1,64,512]{4,3,0,2,1:T(8,128)(2,1)} %copy.170), calls=%async_computation.3 | async-start | bytes 2097152 | tf_op jit(solution)/shard_map/all_to_all | solution.py:237
  266.6 29.6 %copy-start.17 = (s32[4]{0:T(128)S(1)}, s32[4]{0:T(128)}, u32[]{:S(2)}) copy-start(s32[4]{0:T(128)} %get-tuple-element.204) | copy-start | bytes 52
  290.9 10.3 %copy-start.2 = (bf16[2,8,1,64,512]{4,3,0,2,1:T(8,128)(2,1)}, bf16[2,8,1,64,512]{4,3,0,2,1:T(8,128)(2,1)S(1)}, u32[]{:S(2)}) copy-start(bf16[2,8,1,64,512]{4,3,0,2,1:T(8,128)(2,1)S(1)} %all-to-all-done.3) | copy-start | bytes 3145732
  290.9 29.7 %all-to-all-start.4 = ((bf16[2,8,1,64,512]{4,3,0,2,1:T(8,128)(2,1)}), bf16[2,8,1,64,512]{4,3,0,2,1:T(8,128)(2,1)}, u32[]{:S(2)}, u32[]{:S(2)}) async-start(bf16[2,8,1,64,512]{4,3,0,2,1:T(8,128)(2,1)} %copy.173), calls=%async_computation.4 | async-start | bytes 2097152 | tf_op jit(solution)/shard_map/all_to_all | solution.py:237
  320.6 97.9 %all-to-all-start.5 = ((bf16[2,8,1,64,512]{4,3,0,2,1:T(8,128)(2,1)}), bf16[2,8,1,64,512]{4,3,0,2,1:T(8,128)(2,1)}, u32[]{:S(2)}, u32[]{:S(2)}) async-start(bf16[2,8,1,64,512]{4,3,0,2,1:T(8,128)(2,1)} %copy.176), calls=%async_computation.5 | async-start | bytes 2097152 | tf_op jit(solution)/shard_map/all_to_all | solution.py:237
  325.7 85.0 %all-reduce.6.cloned.1.call-start = ((), (), s32[]{:S(2)}) async-start(), calls=%async_computation.6 | async-start | bytes 1048576 | tf_op jit(solution)/shard_map/psum | solution.py:227
  327.9 15.9 %collective-permute-start.2 = (bf16[2,64,512]{2,1,0:T(8,128)(2,1)S(1)}, bf16[2,64,512]{2,1,0:T(8,128)(2,1)}, u32[]{:S(2)}, u32[]{:S(2)}) collective-permute-start(bf16[2,64,512]{2,1,0:T(8,128)(2,1)S(1)} %get-tuple-element.184), channel_id=1, source_target_pairs={{0,1},{1,2},{2,3},{3,4},{4,5},{5,6},{6,7},{8,9},{9,10},{10,11},{11... | collective-permute-start | bytes 393224 | tf_op jit(solution)/shard_map/ppermute | solution.py:20
  331.6 12.2 %collective-permute-start.3 = (bf16[2,64,512]{2,1,0:T(8,128)(2,1)}, bf16[2,64,512]{2,1,0:T(8,128)(2,1)}, u32[]{:S(2)}, u32[]{:S(2)}) collective-permute-start(bf16[2,64,512]{2,1,0:T(8,128)(2,1)} %get-tuple-element.185), channel_id=1, source_target_pairs={{1,0},{2,1},{3,2},{4,3},{5,4},{6,5},{7,6},{9,8},{10,9},{11,10},{12... | collective-permute-start | bytes 393224 | tf_op jit(solution)/shard_map/ppermute | solution.py:21
  343.7 69.7 %copy-start.6 = (pred[8]{0:T(512)(128)(4,1)S(1)}, pred[8]{0:T(512)(128)(4,1)}, u32[]{:S(2)}) copy-start(pred[8]{0:T(512)(128)(4,1)} %copy-done.5) | copy-start | bytes 28
  343.8 69.7 %copy-start.12 = (s32[8]{0:T(128)S(1)}, s32[8]{0:T(128)}, u32[]{:S(2)}) copy-start(s32[8]{0:T(128)} %copy-done.11) | copy-start | bytes 100
  349.3 66.1 %copy-start.8 = (pred[8]{0:T(512)(128)(4,1)S(1)}, pred[8]{0:T(512)(128)(4,1)}, u32[]{:S(2)}) copy-start(pred[8]{0:T(512)(128)(4,1)} %copy-done.7) | copy-start | bytes 28
  349.4 66.1 %copy-start.14 = (s32[8]{0:T(128)S(1)}, s32[8]{0:T(128)}, u32[]{:S(2)}) copy-start(s32[8]{0:T(128)} %copy-done.13) | copy-start | bytes 100
  356.8 61.8 %copy-start.10 = (pred[8]{0:T(512)(128)(4,1)S(1)}, pred[8]{0:T(512)(128)(4,1)}, u32[]{:S(2)}) copy-start(pred[8]{0:T(512)(128)(4,1)} %copy-done.9) | copy-start | bytes 28
  356.8 61.8 %copy-start.16 = (s32[8]{0:T(128)S(1)}, s32[8]{0:T(128)}, u32[]{:S(2)}) copy-start(s32[8]{0:T(128)} %copy-done.15) | copy-start | bytes 100
  421.4 33.0 %collective-permute-start.4 = (bf16[256,5120]{1,0:T(8,128)(2,1)S(1)}, bf16[256,5120]{1,0:T(8,128)(2,1)S(1)}, u32[]{:S(2)}, u32[]{:S(2)}) collective-permute-start(bf16[256,5120]{1,0:T(8,128)(2,1)S(1)} %pad_maximum_fusion), channel_id=1, source_target_pairs={{8,0},{16,8},{24,16},{0,24},{9,1},{17,9},{25,17},{1,25},{10,2},{18... | collective-permute-start | bytes 7864328 | tf_op jit(solution)/shard_map/ppermute | solution.py:34
Sparse Core Ops, SparseCore 0:
  30.9 86.1 all-reduce.7
  334.3 76.4 all-reduce.5
where the time goes:
time: 465 us; the launch traced here: 463 us
  waiting for transfers between devices  185 us (40%)
  local copies, waits for them, and re-layouts  112 us (24%)
  matrix products  73.1 us (16%)
  starting transfers between devices  43.5 us (9%)
  other arithmetic  30.4 us (7%)
  between operations  19.9 us (4%)
    psum x1, waiting for transfers between devices, body(): global_total = lax.psum(global_part, 'seq')  54 us
    all_to_all x3, waiting for transfers between devices, body(): lax.all_to_all(place_terms(random_terms[:, :, slot_num], slot_plans[slot_...  41.7 us
    all_to_all x3, waiting for transfers between devices, body(): lax.all_to_all(serve_tiles(own_blocks, slot_plan), 'seq', split_axis=1, c...  37.1 us
    ppermute x1, waiting for transfers between devices, from_behind(): return lax.ppermute(block, axis, route)  30.4 us
    unnamed x56, local copies, waits for them, and re-layouts  24.8 us
    psum x1, waiting for transfers between devices, broadcast(): return lax.psum(jnp.where(mine, array, jnp.zeros_like(array)), axis)  21.6 us
    all_to_all x3, starting transfers between devices, body(): lax.all_to_all(serve_tiles(own_blocks, slot_plan), 'seq', split_axis=1, c...  16.5 us
    another operation x3, local copies, waits for them, and re-layouts, body(): contrib = jnp.stack([key_terms, value_terms])  15.8 us
  transfers between devices with their start and end apart: 13, of which 7 were waited for; matrix products, arithmetic and copies ran while one was open for 15% of the time, Pallas kernels for 0%

commit v1 on v0

--- a/solution.py
+++ b/solution.py
@@ -8,6 +8,18 @@
 BLK = 64
 GLOB = 2
 RAND = 3
+
+
+def sent_to_each(x, axis, split, join):
+    ways, here = (lax.axis_size(axis), lax.axis_index(axis))
+    width = x.shape[split] // ways
+    turned = jnp.roll(x, -here * width, axis=split)
+    got = [lax.slice_in_dim(turned, 0, width, axis=split)]
+    for far in range(1, ways):
+        sent = lax.slice_in_dim(turned, far * width, (far + 1) * width, axis=split)
+        got.append(lax.ppermute(sent, axis, [(d, (d + far) % ways) for d in range(ways)]))
+    line = jnp.concatenate(got[::-1], axis=join)
+    return jnp.roll(line, (here + 1) * got[0].shape[join], axis=join)
 
 
 def extended_2(array, sides, width):
@@ -234,12 +246,8 @@
     )
     random_terms = contrib[:, :, near:].astype(jnp.bfloat16)
     for slot_num in range(RAND):
-        returned = lax.all_to_all(
-            place_terms(random_terms[:, :, slot_num], slot_plans[slot_num]),
-            "seq",
-            split_axis=1,
-            concat_axis=1,
-            tiled=True,
+        returned = sent_to_each(
+            place_terms(random_terms[:, :, slot_num], slot_plans[slot_num]), "seq", 1, 1
         )
         local_sum = local_sum + absorb_terms(returned, slot_plans[slot_num], query_blocks)
     key_grad = local_sum[0].reshape(shard_tokens, kwidth).astype(jnp.bfloat16)

time: 465 us -> 430 us (0.925)
  waiting for transfers between devices: 185 us -> 126 us
  starting transfers between devices: 43.5 us -> 56.1 us
  other arithmetic: 30.4 us -> 36.1 us
  local copies, waits for them, and re-layouts: 112 us -> 117 us
    psum x1, waiting for transfers between devices: 54 us -> 0.01 us  [body(): global_total = lax.psum(global_part, 'seq')]
    all_to_all x3 -> x0, waiting for transfers between devices: 41.7 us -> none  [body(): lax.all_to_all(place_terms(random_terms[:, :, slot_num], slot_plans[slot_...]
    ppermute x0 -> x21, waiting for transfers between devices: none -> 38.6 us  [sent_to_each(): lax.ppermute(sent, axis, [(d, (d + far) % ways) for d in range(ways)])]
    ppermute x0 -> x21, starting transfers between devices: none -> 28.5 us  [sent_to_each(): lax.ppermute(sent, axis, [(d, (d + far) % ways) for d in range(ways)])]
    all_to_all x3 -> x0, starting transfers between devices: 13.9 us -> none  [body(): lax.all_to_all(place_terms(random_terms[:, :, slot_num], slot_plans[slot_...]
    concatenate x0 -> x6, other arithmetic: none -> 6.79 us  [the longest x3 5.61 us: sent_to_each(): return jnp.roll(line, (here + 1) * got[0].shape[join], axis=join)]
    unnamed x56 -> x107, local copies, waits for them, and re-layouts: 24.8 us -> 30.3 us
  transfers between devices with their start and end apart: 13 -> 31, of which waited for: 7 -> 10; matrix products, arithmetic and copies ran while one was open for 15% -> 16% of each run, Pallas kernels for 0% -> 0%
where the time goes in v1:
time: 430 us; the launch traced here: 426 us
  waiting for transfers between devices  126 us (29%)
  local copies, waits for them, and re-layouts  117 us (27%)
  matrix products  69.2 us (16%)
  starting transfers between devices  56.1 us (13%)
  other arithmetic  36.1 us (8%)
  between operations  20.6 us (5%)
    ppermute x21, waiting for transfers between devices, sent_to_each(): lax.ppermute(sent, axis, [(d, (d + far) % ways) for d in range(ways)])  38.6 us
    all_to_all x3, waiting for transfers between devices, body(): lax.all_to_all(serve_tiles(own_blocks, slot_plan), 'seq', split_axis=1, c...  36.1 us
    unnamed x107, local copies, waits for them, and re-layouts  30.3 us
    ppermute x1, waiting for transfers between devices, from_behind(): return lax.ppermute(block, axis, route)  30.2 us
    ppermute x21, starting transfers between devices, sent_to_each(): lax.ppermute(sent, axis, [(d, (d + far) % ways) for d in range(ways)])  28.5 us
    psum x1, waiting for transfers between devices, broadcast(): return lax.psum(jnp.where(mine, array, jnp.zeros_like(array)), axis)  21.3 us
    all_to_all x3, starting transfers between devices, body(): lax.all_to_all(serve_tiles(own_blocks, slot_plan), 'seq', split_axis=1, c...  16.5 us
    another operation x3, local copies, waits for them, and re-layouts, body(): contrib = jnp.stack([key_terms, value_terms])  15.9 us
  transfers between devices with their start and end apart: 31, of which 10 were waited for; matrix products, arithmetic and copies ran while one was open for 16% of the time, Pallas kernels for 0%

profile of v1, /device:TPU:1, one launch (start us, length us, event | category | flops | bytes accessed | tf_op | source)
XLA Modules:
  0.0 426.2 jit_solution(1402539442485163130)
XLA Ops:
  9.2 4.0 collective-permute-start
  17.7 6.4 %all-to-all-start = ((bf16[2,8,1,64,512]{4,3,0,2,1:T(8,128)(2,1)}), bf16[2,8,1,64,512]{4,3,0,2,1:T(8,128)(2,1)S(1)}, u32[]{:S(2)}, u32[]{:S(2)}) async-start(bf16[2,8,1,64,512]{4,3,0,2,1:T(8,128)(2,1)} %fusion.60), calls=%async_computation | async-start | bytes 2097152 | tf_op jit(solution)/shard_map/all_to_all | solution.py:208
  34.2 16.8 %all-to-all-done = bf16[2,8,1,64,512]{4,3,0,2,1:T(8,128)(2,1)S(1)} async-done(((bf16[2,8,1,64,512]{4,3,0,2,1:T(8,128)(2,1)}), bf16[2,8,1,64,512]{4,3,0,2,1:T(8,128)(2,1)S(1)}, u32[]{:S(2)}, u32[]{:S(2)}) %all-to-all-start) | async-done | bytes 1048608 | tf_op jit(solution)/shard_map/all_to_all | solution.py:208
  51.1 5.3 %all-to-all-start.1 = ((bf16[2,8,1,64,512]{4,3,0,2,1:T(8,128)(2,1)}), bf16[2,8,1,64,512]{4,3,0,2,1:T(8,128)(2,1)S(1)}, u32[]{:S(2)}, u32[]{:S(2)}) async-start(bf16[2,8,1,64,512]{4,3,0,2,1:T(8,128)(2,1)} %fusion.59), calls=%async_computation.1 | async-start | bytes 2097152 | tf_op jit(solution)/shard_map/all_to_all | solution.py:208
  62.7 19.2 %all-to-all-done.1 = bf16[2,8,1,64,512]{4,3,0,2,1:T(8,128)(2,1)S(1)} async-done(((bf16[2,8,1,64,512]{4,3,0,2,1:T(8,128)(2,1)}), bf16[2,8,1,64,512]{4,3,0,2,1:T(8,128)(2,1)S(1)}, u32[]{:S(2)}, u32[]{:S(2)}) %all-to-all-start.1) | async-done | bytes 1048608 | tf_op jit(solution)/shard_map/all_to_all | solution.py:208
  82.0 4.8 %all-to-all-start.2 = ((bf16[2,8,1,64,512]{4,3,0,2,1:T(8,128)(2,1)}), bf16[2,8,1,64,512]{4,3,0,2,1:T(8,128)(2,1)}, u32[]{:S(2)}, u32[]{:S(2)}) async-start(bf16[2,8,1,64,512]{4,3,0,2,1:T(8,128)(2,1)} %fusion.58), calls=%async_computation.2 | async-start | bytes 2097152 | tf_op jit(solution)/shard_map/all_to_all | solution.py:208
  87.7 3.5 copy.195
  95.6 21.3 %all-reduce.8.cloned.1.call-done = (bf16[2,1,64,512]{3,2,1,0:T(8,128)(2,1)}, bf16[2,1,64,512]{3,2,1,0:T(8,128)(2,1)}) async-done(((bf16[2,1,64,512]{3,2,1,0:T(8,128)(2,1)}, bf16[2,1,64,512]{3,2,1,0:T(8,128)(2,1)}), (bf16[2,1,64,512]{3,2,1,0:T(8,128)(2,1)}, bf16[2,1,64,512]{3,2,1,0:T(8,128)(2,1)})) %all-reduce.8.cloned.1.call-update) | async-done | bytes 262160 | tf_op jit(solution)/shard_map/psum | solution.py:40
  127.2 4.0 fusion.136
  135.3 4.0 reshape_squeeze.13
  139.4 3.5 copy.157
  142.9 77.9 %while.17 = (s32[]{:T(128)}, bf16[4,4,64,8,128]{4,2,3,1,0:T(8,128)(2,1)}, f32[4,4,8,64,128]{4,3,2,1,0:T(8,128)}, f32[4,4,8,64,128]{4,3,2,1,0:T(8,128)}, bf16[4,4...) while((s32[]{:T(128)}, ...), condition=%wide.region_16.18_spmd.clone, body=%wide.region_12.17_spmd.clone.sunk | while | flops 1633945600 | bytes 56234432 | solution.py:102
  148.6 3.6 fusion.180
  152.2 2.9 fusion.176
  155.1 3.0 fusion.177
  168.0 3.6 fusion.180
  171.5 2.9 fusion.176
  174.5 3.0 fusion.177
  187.3 3.5 fusion.180
  190.8 2.9 fusion.176
  193.8 3.0 fusion.177
  206.6 3.6 fusion.180
  210.2 2.9 fusion.176
  213.1 3.0 fusion.177
  220.8 7.8 %copy.160 = f32[4,8,64,4,128]{4,3,2,0,1:T(4,128)} copy(f32[4,8,64,4,128]{4,2,1,0,3:T(8,128)} %bitcast.563) | data formatting | bytes 8388608 | tf_op jit(solution)/shard_map/transpose | solution.py:107
  228.6 5.5 %stack_reshape.6 = f32[1,4,8,64,512]{4,3,0,1,2:T(8,128)} reshape(f32[4,8,64,4,128]{4,3,2,0,1:T(4,128)} %copy.160) | data formatting | bytes 8388608 | tf_op jit(solution)/shard_map/stack;reshape | solution.py:230
  234.0 5.0 %constant_dynamic-update-slice_fusion.3 = f32[2,4,8,64,512]{4,3,0,1,2:T(8,128)} fusion(f32[1,4,8,64,512]{4,3,0,1,2:T(8,128)} %stack_reshape.6), kind=kLoop, calls=%fused_computation.145 | loop fusion | bytes 8388608
  239.0 5.5 %copy.161 = f32[4,8,64,4,128]{4,3,2,0,1:T(4,128)} copy(f32[4,8,64,4,128]{4,2,1,0,3:T(8,128)S(1)} %bitcast.564) | data formatting | bytes 8388608 | tf_op jit(solution)/shard_map/transpose | solution.py:108
  244.6 5.5 %stack_reshape.7 = f32[1,4,8,64,512]{4,3,0,1,2:T(8,128)} reshape(f32[4,8,64,4,128]{4,3,2,0,1:T(4,128)} %copy.161) | data formatting | bytes 8388608 | tf_op jit(solution)/shard_map/stack;reshape | solution.py:230
  250.1 4.9 %constant_dynamic-update-slice_fusion.2 = f32[2,4,8,64,512]{4,3,0,1,2:T(8,128)} fusion(f32[2,4,8,64,512]{4,3,0,1,2:T(8,128)} %constant_dynamic-update-slice_fusion.3, f32[1,4,8,64,512]{4,3,0,1,2:T(8,128)} %stack_reshape.7), kind=kLoop, calls=%fused_computation.144 | loop fusion | bytes 8388608 | tf_op jit(solution)/shard_map/stack | solution.py:230
  255.0 4.0 convert.13
  271.7 3.1 collective-permute-start.2
  277.4 4.3 %copy.159 = bf16[4,64,4,8,128]{4,3,2,1,0:T(8,128)(2,1)} copy(bf16[4,64,4,8,128]{4,1,3,0,2:T(8,128)(2,1)} %bitcast.479) | data formatting | bytes 4194304 | tf_op jit(solution)/shard_map/convert_element_type | solution.py:255
  281.7 2.8 convert_element_type.53
  286.8 4.4 %collective-permute-start.21 = (bf16[2,1,1,64,512]{4,3,1,0,2:T(8,128)(2,1)S(1)}, bf16[2,1,1,64,512]{4,3,1,0,2:T(8,128)(2,1)S(1)}, u32[]{:S(2)}, u32[]{:S(2)}) collective-permute-start(bf16[2,1,1,64,512]{4,3,1,0,2:T(8,128)(2,1)S(1)} %copy-done.18), channel_id=1, source_target_pairs={{0,4},{1,5},{2,6},{3,7},{4,0},{5,1},{6,2},{7,3},{8,12},{9,13},{10,... | collective-permute-start | bytes 393224 | tf_op jit(solution)/shard_map/ppermute | solution.py:20
  300.6 4.2 collective-permute-done.21
  304.8 8.3 %collective-permute-done.22 = bf16[2,1,1,64,512]{4,3,1,0,2:T(8,128)(2,1)S(1)} collective-permute-done((bf16[2,1,1,64,512]{4,3,1,0,2:T(8,128)(2,1)S(1)}, bf16[2,1,1,64,512]{4,3,1,0,2:T(8,128)(2,1)S(1)}, u32[]{:S(2)}, u32[]{:S(2)}) %collective-permute-start.22) | collective-permute-done | bytes 131104 | tf_op jit(solution)/shard_map/ppermute | solution.py:20
  318.1 3.0 collective-permute-start.4
  321.1 8.3 %collective-permute-done.14 = bf16[2,1,1,64,512]{4,3,1,0,2:T(8,128)(2,1)S(1)} collective-permute-done((bf16[2,1,1,64,512]{4,3,1,0,2:T(8,128)(2,1)S(1)}, bf16[2,1,1,64,512]{4,3,1,0,2:T(8,128)(2,1)S(1)}, u32[]{:S(2)}, u32[]{:S(2)}) %collective-permute-start.14) | collective-permute-done | bytes 131104 | tf_op jit(solution)/shard_map/ppermute | solution.py:20
  329.4 6.4 %collective-permute-done.15 = bf16[2,1,1,64,512]{4,3,1,0,2:T(8,128)(2,1)S(1)} collective-permute-done((bf16[2,1,1,64,512]{4,3,1,0,2:T(8,128)(2,1)S(1)}, bf16[2,1,1,64,512]{4,3,1,0,2:T(8,128)(2,1)S(1)}, u32[]{:S(2)}, u32[]{:S(2)}) %collective-permute-start.15) | collective-permute-done | bytes 131104 | tf_op jit(solution)/shard_map/ppermute | solution.py:20
  336.0 7.2 %collective-permute-start.8 = (bf16[2,1,1,64,512]{4,3,1,0,2:T(8,128)(2,1)S(1)}, bf16[2,1,1,64,512]{4,3,1,0,2:T(8,128)(2,1)S(1)}, u32[]{:S(2)}, u32[]{:S(2)}) collective-permute-start(bf16[2,1,1,64,512]{4,3,1,0,2:T(8,128)(2,1)S(1)} %get-tuple-element.207), channel_id=1, source_target_pairs={{0,3},{1,4},{2,5},{3,6},{4,7},{5,0},{6,1},{7,2},{8,11},{9,12},{10,... | collective-permute-start | bytes 393224 | tf_op jit(solution)/shard_map/ppermute | solution.py:20
  344.9 3.1 collective-permute-start.10
  349.3 5.7 %collective-permute-done.7 = bf16[2,1,1,64,512]{4,3,1,0,2:T(8,128)(2,1)S(1)} collective-permute-done((bf16[2,1,1,64,512]{4,3,1,0,2:T(8,128)(2,1)S(1)}, bf16[2,1,1,64,512]{4,3,1,0,2:T(8,128)(2,1)S(1)}, u32[]{:S(2)}, u32[]{:S(2)}) %collective-permute-start.7) | collective-permute-done | bytes 131104 | tf_op jit(solution)/shard_map/ppermute | solution.py:20
  355.7 5.6 %collective-permute-done.8 = bf16[2,1,1,64,512]{4,3,1,0,2:T(8,128)(2,1)S(1)} collective-permute-done((bf16[2,1,1,64,512]{4,3,1,0,2:T(8,128)(2,1)S(1)}, bf16[2,1,1,64,512]{4,3,1,0,2:T(8,128)(2,1)S(1)}, u32[]{:S(2)}, u32[]{:S(2)}) %collective-permute-start.8) | collective-permute-done | bytes 131104 | tf_op jit(solution)/shard_map/ppermute | solution.py:20
  365.3 6.3 %scatter-add.9 = f32[2,4,64,512]{3,1,2,0:T(4,128)} dynamic-update-slice(f32[2,4,64,512]{3,1,2,0:T(4,128)} %copy.164, f32[2,1,64,512]{3,1,2,0:T(1,128)S(1)} %copy_add_fusion, s32[]{:T(128)} %constant.259.clone.1, s32[]{:T(128)} %constant.263.clone.1, s32[]{:T(128)} %constant.259.clone.1, s32[]{:T(128)} %constant.259.clone.1) | dynamic-update-slice | bytes 524292 | tf_op jit(solution)/shard_map/scatter-add | solution.py:237
  371.6 2.6 fusion.49
  378.4 2.7 fusion.45
  386.6 30.2 %collective-permute-done.25 = bf16[256,5120]{1,0:T(8,128)(2,1)S(1)} collective-permute-done((bf16[256,5120]{1,0:T(8,128)(2,1)S(1)}, bf16[256,5120]{1,0:T(8,128)(2,1)S(1)}, u32[]{:S(2)}, u32[]{:S(2)}) %collective-permute-start.25) | collective-permute-done | bytes 2621472 | tf_op jit(solution)/shard_map/ppermute | solution.py:46
  (294 shorter events, 127.4 us)
Async XLA Ops:
  7.2 17.0 %copy-start.34 = (s32[1,2]{1,0:T(1,128)S(1)}, s32[1,2]{1,0:T(1,128)}, u32[]{:S(2)}) copy-start(s32[1,2]{1,0:T(1,128)} %param.22) | copy-start | bytes 28
  9.2 83.9 %collective-permute-start = (bf16[2,64,512]{2,1,0:T(8,128)(2,1)S(1)}, bf16[2,64,512]{2,1,0:T(8,128)(2,1)S(1)}, u32[]{:S(2)}, u32[]{:S(2)}) collective-permute-start(bf16[2,64,512]{2,1,0:T(8,128)(2,1)S(1)} %get-tuple-element.216), channel_id=1, source_target_pairs={{0,1},{1,2},{2,3},{3,4},{4,5},{5,6},{6,7},{8,9},{9,10},{10,11},{11... | collective-permute-start | bytes 393224 | tf_op jit(solution)/shard_map/ppermute | solution.py:32
  13.1 79.9 %collective-permute-start.1 = (bf16[2,64,512]{2,1,0:T(8,128)(2,1)S(1)}, bf16[2,64,512]{2,1,0:T(8,128)(2,1)S(1)}, u32[]{:S(2)}, u32[]{:S(2)}) collective-permute-start(bf16[2,64,512]{2,1,0:T(8,128)(2,1)S(1)} %get-tuple-element.217), channel_id=1, source_target_pairs={{1,0},{2,1},{3,2},{4,3},{5,4},{6,5},{7,6},{9,8},{10,9},{11,10},{12... | collective-permute-start | bytes 393224 | tf_op jit(solution)/shard_map/ppermute | solution.py:33
  15.9 15.9 %copy-start.19 = (pred[8]{0:T(512)(128)(4,1)}, pred[8]{0:T(512)(128)(4,1)S(1)}, u32[]{:S(2)}) copy-start(pred[8]{0:T(512)(128)(4,1)S(1)} %get-tuple-element.174) | copy-start | bytes 28
  15.9 15.9 %copy-start.25 = (s32[8]{0:T(128)}, s32[8]{0:T(128)S(1)}, u32[]{:S(2)}) copy-start(s32[8]{0:T(128)S(1)} %fusion.79) | copy-start | bytes 100
  17.7 33.3 %all-to-all-start = ((bf16[2,8,1,64,512]{4,3,0,2,1:T(8,128)(2,1)}), bf16[2,8,1,64,512]{4,3,0,2,1:T(8,128)(2,1)S(1)}, u32[]{:S(2)}, u32[]{:S(2)}) async-start(bf16[2,8,1,64,512]{4,3,0,2,1:T(8,128)(2,1)} %fusion.60), calls=%async_computation | async-start | bytes 2097152 | tf_op jit(solution)/shard_map/all_to_all | solution.py:208
  24.1 92.8 %all-reduce.8.cloned.1.call-start = ((), (), s32[]{:S(2)}) async-start(), calls=%async_computation.4 | async-start | bytes 524288 | tf_op jit(solution)/shard_map/psum | solution.py:40
  31.1 26.8 %copy-start.21 = (pred[8]{0:T(512)(128)(4,1)}, pred[8]{0:T(512)(128)(4,1)S(1)}, u32[]{:S(2)}) copy-start(pred[8]{0:T(512)(128)(4,1)S(1)} %get-tuple-element.172) | copy-start | bytes 28
  31.8 26.1 %copy-start.27 = (s32[8]{0:T(128)}, s32[8]{0:T(128)S(1)}, u32[]{:S(2)}) copy-start(s32[8]{0:T(128)S(1)} %fusion.83) | copy-start | bytes 100
  31.8 26.1 %copy-start.37 = (s32[1,8]{1,0:T(1,128)S(1)}, s32[1,8]{1,0:T(1,128)}, u32[]{:S(2)}) copy-start(s32[1,8]{1,0:T(1,128)} %param.23) | copy-start | bytes 100
  32.8 29.9 %copy-start.23 = (pred[8]{0:T(512)(128)(4,1)}, pred[8]{0:T(512)(128)(4,1)S(1)}, u32[]{:S(2)}) copy-start(pred[8]{0:T(512)(128)(4,1)S(1)} %get-tuple-element.170) | copy-start | bytes 28
  32.9 29.9 %copy-start.29 = (s32[8]{0:T(128)}, s32[8]{0:T(128)S(1)}, u32[]{:S(2)}) copy-start(s32[8]{0:T(128)S(1)} %fusion.87) | copy-start | bytes 100
  51.1 30.9 %all-to-all-start.1 = ((bf16[2,8,1,64,512]{4,3,0,2,1:T(8,128)(2,1)}), bf16[2,8,1,64,512]{4,3,0,2,1:T(8,128)(2,1)S(1)}, u32[]{:S(2)}, u32[]{:S(2)}) async-start(bf16[2,8,1,64,512]{4,3,0,2,1:T(8,128)(2,1)} %fusion.59), calls=%async_computation.1 | async-start | bytes 2097152 | tf_op jit(solution)/shard_map/all_to_all | solution.py:208
  82.0 42.4 %all-to-all-start.2 = ((bf16[2,8,1,64,512]{4,3,0,2,1:T(8,128)(2,1)}), bf16[2,8,1,64,512]{4,3,0,2,1:T(8,128)(2,1)}, u32[]{:S(2)}, u32[]{:S(2)}) async-start(bf16[2,8,1,64,512]{4,3,0,2,1:T(8,128)(2,1)} %fusion.58), calls=%async_computation.2 | async-start | bytes 2097152 | tf_op jit(solution)/shard_map/all_to_all | solution.py:208
  86.8 291.6 %all-reduce.6.cloned.1.call-start = ((), (), s32[]{:S(2)}) async-start(), calls=%async_computation.3 | async-start | bytes 1048576 | tf_op jit(solution)/shard_map/psum | solution.py:239
  265.9 26.8 %collective-permute-start.18 = (bf16[2,1,1,64,512]{4,3,1,0,2:T(8,128)(2,1)}, bf16[2,1,1,64,512]{4,3,1,0,2:T(8,128)(2,1)}, u32[]{:S(2)}, u32[]{:S(2)}) collective-permute-start(bf16[2,1,1,64,512]{4,3,1,0,2:T(8,128)(2,1)} %get-tuple-element.197), channel_id=1, source_target_pairs={{0,7},{1,0},{2,1},{3,2},{4,3},{5,4},{6,5},{7,6},{8,15},{9,8},{10,9... | collective-permute-start | bytes 393224 | tf_op jit(solution)/shard_map/ppermute | solution.py:20
  267.7 26.7 %collective-permute-start.19 = (bf16[2,1,1,64,512]{4,3,1,0,2:T(8,128)(2,1)}, bf16[2,1,1,64,512]{4,3,1,0,2:T(8,128)(2,1)}, u32[]{:S(2)}, u32[]{:S(2)}) collective-permute-start(bf16[2,1,1,64,512]{4,3,1,0,2:T(8,128)(2,1)} %get-tuple-element.196), channel_id=1, source_target_pairs={{0,6},{1,7},{2,0},{3,1},{4,2},{5,3},{6,4},{7,5},{8,14},{9,15},{10,... | collective-permute-start | bytes 393224 | tf_op jit(solution)/shard_map/ppermute | solution.py:20
  267.7 29.5 %collective-permute-start.20 = (bf16[2,1,1,64,512]{4,3,1,0,2:T(8,128)(2,1)}, bf16[2,1,1,64,512]{4,3,1,0,2:T(8,128)(2,1)}, u32[]{:S(2)}, u32[]{:S(2)}) collective-permute-start(bf16[2,1,1,64,512]{4,3,1,0,2:T(8,128)(2,1)} %get-tuple-element.195), channel_id=1, source_target_pairs={{0,5},{1,6},{2,7},{3,0},{4,1},{5,2},{6,3},{7,4},{8,13},{9,14},{10,... | collective-permute-start | bytes 393224 | tf_op jit(solution)/shard_map/ppermute | solution.py:20
  271.7 15.1 %collective-permute-start.2 = (bf16[2,64,512]{2,1,0:T(8,128)(2,1)S(1)}, bf16[2,64,512]{2,1,0:T(8,128)(2,1)S(1)}, u32[]{:S(2)}, u32[]{:S(2)}) collective-permute-start(bf16[2,64,512]{2,1,0:T(8,128)(2,1)S(1)} %get-tuple-element.185), channel_id=1, source_target_pairs={{0,1},{1,2},{2,3},{3,4},{4,5},{5,6},{6,7},{8,9},{9,10},{10,11},{11... | collective-permute-start | bytes 393224 | tf_op jit(solution)/shard_map/ppermute | solution.py:32
  274.9 16.4 %collective-permute-start.3 = (bf16[2,64,512]{2,1,0:T(8,128)(2,1)S(1)}, bf16[2,64,512]{2,1,0:T(8,128)(2,1)}, u32[]{:S(2)}, u32[]{:S(2)}) collective-permute-start(bf16[2,64,512]{2,1,0:T(8,128)(2,1)S(1)} %get-tuple-element.186), channel_id=1, source_target_pairs={{1,0},{2,1},{3,2},{4,3},{5,4},{6,5},{7,6},{9,8},{10,9},{11,10},{12... | collective-permute-start | bytes 393224 | tf_op jit(solution)/shard_map/ppermute | solution.py:33
  284.6 20.2 %copy-start.13 = (bf16[2,1,1,64,512]{4,3,1,0,2:T(8,128)(2,1)S(1)}, bf16[2,1,1,64,512]{4,3,1,0,2:T(8,128)(2,1)}, u32[]{:S(2)}) copy-start(bf16[2,1,1,64,512]{4,3,1,0,2:T(8,128)(2,1)} %get-tuple-element.203) | copy-start | bytes 393220
  284.6 28.6 %copy-start.12 = (bf16[2,1,1,64,512]{4,3,1,0,2:T(8,128)(2,1)S(1)}, bf16[2,1,1,64,512]{4,3,1,0,2:T(8,128)(2,1)}, u32[]{:S(2)}) copy-start(bf16[2,1,1,64,512]{4,3,1,0,2:T(8,128)(2,1)} %get-tuple-element.202) | copy-start | bytes 393220
  284.6 28.6 %copy-start.11 = (bf16[2,1,1,64,512]{4,3,1,0,2:T(8,128)(2,1)S(1)}, bf16[2,1,1,64,512]{4,3,1,0,2:T(8,128)(2,1)}, u32[]{:S(2)}) copy-start(bf16[2,1,1,64,512]{4,3,1,0,2:T(8,128)(2,1)} %get-tuple-element.201) | copy-start | bytes 393220
  286.7 26.6 %copy-start.10 = (bf16[2,1,1,64,512]{4,3,1,0,2:T(8,128)(2,1)S(1)}, bf16[2,1,1,64,512]{4,3,1,0,2:T(8,128)(2,1)}, u32[]{:S(2)}) copy-start(bf16[2,1,1,64,512]{4,3,1,0,2:T(8,128)(2,1)} %get-tuple-element.200) | copy-start | bytes 393220
  286.7 30.0 %copy-start.9 = (bf16[2,1,1,64,512]{4,3,1,0,2:T(8,128)(2,1)S(1)}, bf16[2,1,1,64,512]{4,3,1,0,2:T(8,128)(2,1)}, u32[]{:S(2)}) copy-start(bf16[2,1,1,64,512]{4,3,1,0,2:T(8,128)(2,1)} %get-tuple-element.199) | copy-start | bytes 393220
  286.7 30.1 %copy-start.8 = (bf16[2,1,1,64,512]{4,3,1,0,2:T(8,128)(2,1)S(1)}, bf16[2,1,1,64,512]{4,3,1,0,2:T(8,128)(2,1)}, u32[]{:S(2)}) copy-start(bf16[2,1,1,64,512]{4,3,1,0,2:T(8,128)(2,1)} %get-tuple-element.198) | copy-start | bytes 393220
  286.8 18.0 %collective-permute-start.21 = (bf16[2,1,1,64,512]{4,3,1,0,2:T(8,128)(2,1)S(1)}, bf16[2,1,1,64,512]{4,3,1,0,2:T(8,128)(2,1)S(1)}, u32[]{:S(2)}, u32[]{:S(2)}) collective-permute-start(bf16[2,1,1,64,512]{4,3,1,0,2:T(8,128)(2,1)S(1)} %copy-done.18), channel_id=1, source_target_pairs={{0,4},{1,5},{2,6},{3,7},{4,0},{5,1},{6,2},{7,3},{8,12},{9,13},{10,... | collective-permute-start | bytes 393224 | tf_op jit(solution)/shard_map/ppermute | solution.py:20
  291.3 21.9 %collective-permute-start.22 = (bf16[2,1,1,64,512]{4,3,1,0,2:T(8,128)(2,1)S(1)}, bf16[2,1,1,64,512]{4,3,1,0,2:T(8,128)(2,1)S(1)}, u32[]{:S(2)}, u32[]{:S(2)}) collective-permute-start(bf16[2,1,1,64,512]{4,3,1,0,2:T(8,128)(2,1)S(1)} %copy-done.17), channel_id=1, source_target_pairs={{0,3},{1,4},{2,5},{3,6},{4,7},{5,0},{6,1},{7,2},{8,11},{9,12},{10,... | collective-permute-start | bytes 393224 | tf_op jit(solution)/shard_map/ppermute | solution.py:20
  292.8 20.4 %collective-permute-start.23 = (bf16[2,1,1,64,512]{4,3,1,0,2:T(8,128)(2,1)S(1)}, bf16[2,1,1,64,512]{4,3,1,0,2:T(8,128)(2,1)S(1)}, u32[]{:S(2)}, u32[]{:S(2)}) collective-permute-start(bf16[2,1,1,64,512]{4,3,1,0,2:T(8,128)(2,1)S(1)} %copy-done.16), channel_id=1, source_target_pairs={{0,2},{1,3},{2,4},{3,5},{4,6},{5,7},{6,0},{7,1},{8,10},{9,11},{10,... | collective-permute-start | bytes 393224 | tf_op jit(solution)/shard_map/ppermute | solution.py:20
  294.5 18.9 %collective-permute-start.24 = (bf16[2,1,1,64,512]{4,3,1,0,2:T(8,128)(2,1)S(1)}, bf16[2,1,1,64,512]{4,3,1,0,2:T(8,128)(2,1)S(1)}, u32[]{:S(2)}, u32[]{:S(2)}) collective-permute-start(bf16[2,1,1,64,512]{4,3,1,0,2:T(8,128)(2,1)S(1)} %copy-done.14), channel_id=1, source_target_pairs={{0,1},{1,2},{2,3},{3,4},{4,5},{5,6},{6,7},{7,0},{8,9},{9,10},{10,1... | collective-permute-start | bytes 393224 | tf_op jit(solution)/shard_map/ppermute | solution.py:20
  297.2 19.5 %collective-permute-start.11 = (bf16[2,1,1,64,512]{4,3,1,0,2:T(8,128)(2,1)S(1)}, bf16[2,1,1,64,512]{4,3,1,0,2:T(8,128)(2,1)S(1)}, u32[]{:S(2)}, u32[]{:S(2)}) collective-permute-start(bf16[2,1,1,64,512]{4,3,1,0,2:T(8,128)(2,1)S(1)} %copy-done.15), channel_id=1, source_target_pairs={{0,7},{1,0},{2,1},{3,2},{4,3},{5,4},{6,5},{7,6},{8,15},{9,8},{10,9... | collective-permute-start | bytes 393224 | tf_op jit(solution)/shard_map/ppermute | solution.py:20
  304.8 12.0 %collective-permute-start.12 = (bf16[2,1,1,64,512]{4,3,1,0,2:T(8,128)(2,1)S(1)}, bf16[2,1,1,64,512]{4,3,1,0,2:T(8,128)(2,1)S(1)}, u32[]{:S(2)}, u32[]{:S(2)}) collective-permute-start(bf16[2,1,1,64,512]{4,3,1,0,2:T(8,128)(2,1)S(1)} %copy-done.13), channel_id=1, source_target_pairs={{0,6},{1,7},{2,0},{3,1},{4,2},{5,3},{6,4},{7,5},{8,14},{9,15},{10,... | collective-permute-start | bytes 393224 | tf_op jit(solution)/shard_map/ppermute | solution.py:20
  313.2 4.9 %collective-permute-start.13 = (bf16[2,1,1,64,512]{4,3,1,0,2:T(8,128)(2,1)S(1)}, bf16[2,1,1,64,512]{4,3,1,0,2:T(8,128)(2,1)S(1)}, u32[]{:S(2)}, u32[]{:S(2)}) collective-permute-start(bf16[2,1,1,64,512]{4,3,1,0,2:T(8,128)(2,1)S(1)} %copy-done.12), channel_id=1, source_target_pairs={{0,5},{1,6},{2,7},{3,0},{4,1},{5,2},{6,3},{7,4},{8,13},{9,14},{10,... | collective-permute-start | bytes 393224 | tf_op jit(solution)/shard_map/ppermute | solution.py:20
  313.2 16.2 %collective-permute-start.14 = (bf16[2,1,1,64,512]{4,3,1,0,2:T(8,128)(2,1)S(1)}, bf16[2,1,1,64,512]{4,3,1,0,2:T(8,128)(2,1)S(1)}, u32[]{:S(2)}, u32[]{:S(2)}) collective-permute-start(bf16[2,1,1,64,512]{4,3,1,0,2:T(8,128)(2,1)S(1)} %copy-done.11), channel_id=1, source_target_pairs={{0,4},{1,5},{2,6},{3,7},{4,0},{5,1},{6,2},{7,3},{8,12},{9,13},{10,... | collective-permute-start | bytes 393224 | tf_op jit(solution)/shard_map/ppermute | solution.py:20
  313.3 22.5 %collective-permute-start.15 = (bf16[2,1,1,64,512]{4,3,1,0,2:T(8,128)(2,1)S(1)}, bf16[2,1,1,64,512]{4,3,1,0,2:T(8,128)(2,1)S(1)}, u32[]{:S(2)}, u32[]{:S(2)}) collective-permute-start(bf16[2,1,1,64,512]{4,3,1,0,2:T(8,128)(2,1)S(1)} %copy-done.10), channel_id=1, source_target_pairs={{0,3},{1,4},{2,5},{3,6},{4,7},{5,0},{6,1},{7,2},{8,11},{9,12},{10,... | collective-permute-start | bytes 393224 | tf_op jit(solution)/shard_map/ppermute | solution.py:20
  316.7 19.2 %collective-permute-start.16 = (bf16[2,1,1,64,512]{4,3,1,0,2:T(8,128)(2,1)S(1)}, bf16[2,1,1,64,512]{4,3,1,0,2:T(8,128)(2,1)S(1)}, u32[]{:S(2)}, u32[]{:S(2)}) collective-permute-start(bf16[2,1,1,64,512]{4,3,1,0,2:T(8,128)(2,1)S(1)} %copy-done.9), channel_id=1, source_target_pairs={{0,2},{1,3},{2,4},{3,5},{4,6},{5,7},{6,0},{7,1},{8,10},{9,11},{10,... | collective-permute-start | bytes 393224 | tf_op jit(solution)/shard_map/ppermute | solution.py:20
  316.8 19.2 %collective-permute-start.17 = (bf16[2,1,1,64,512]{4,3,1,0,2:T(8,128)(2,1)S(1)}, bf16[2,1,1,64,512]{4,3,1,0,2:T(8,128)(2,1)S(1)}, u32[]{:S(2)}, u32[]{:S(2)}) collective-permute-start(bf16[2,1,1,64,512]{4,3,1,0,2:T(8,128)(2,1)S(1)} %copy-done.8), channel_id=1, source_target_pairs={{0,1},{1,2},{2,3},{3,4},{4,5},{5,6},{6,7},{7,0},{8,9},{9,10},{10,1... | collective-permute-start | bytes 393224 | tf_op jit(solution)/shard_map/ppermute | solution.py:20
  318.1 26.0 %collective-permute-start.4 = (bf16[2,1,1,64,512]{4,3,1,0,2:T(8,128)(2,1)S(1)}, bf16[2,1,1,64,512]{4,3,1,0,2:T(8,128)(2,1)S(1)}, u32[]{:S(2)}, u32[]{:S(2)}) collective-permute-start(bf16[2,1,1,64,512]{4,3,1,0,2:T(8,128)(2,1)S(1)} %get-tuple-element.211), channel_id=1, source_target_pairs={{0,7},{1,0},{2,1},{3,2},{4,3},{5,4},{6,5},{7,6},{8,15},{9,8},{10,9... | collective-permute-start | bytes 393224 | tf_op jit(solution)/shard_map/ppermute | solution.py:20
  329.4 15.5 %collective-permute-start.5 = (bf16[2,1,1,64,512]{4,3,1,0,2:T(8,128)(2,1)S(1)}, bf16[2,1,1,64,512]{4,3,1,0,2:T(8,128)(2,1)S(1)}, u32[]{:S(2)}, u32[]{:S(2)}) collective-permute-start(bf16[2,1,1,64,512]{4,3,1,0,2:T(8,128)(2,1)S(1)} %get-tuple-element.210), channel_id=1, source_target_pairs={{0,6},{1,7},{2,0},{3,1},{4,2},{5,3},{6,4},{7,5},{8,14},{9,15},{10,... | collective-permute-start | bytes 393224 | tf_op jit(solution)/shard_map/ppermute | solution.py:20
  335.8 12.8 %collective-permute-start.6 = (bf16[2,1,1,64,512]{4,3,1,0,2:T(8,128)(2,1)S(1)}, bf16[2,1,1,64,512]{4,3,1,0,2:T(8,128)(2,1)S(1)}, u32[]{:S(2)}, u32[]{:S(2)}) collective-permute-start(bf16[2,1,1,64,512]{4,3,1,0,2:T(8,128)(2,1)S(1)} %get-tuple-element.209), channel_id=1, source_target_pairs={{0,5},{1,6},{2,7},{3,0},{4,1},{5,2},{6,3},{7,4},{8,13},{9,14},{10,... | collective-permute-start | bytes 393224 | tf_op jit(solution)/shard_map/ppermute | solution.py:20
  335.9 19.2 %collective-permute-start.7 = (bf16[2,1,1,64,512]{4,3,1,0,2:T(8,128)(2,1)S(1)}, bf16[2,1,1,64,512]{4,3,1,0,2:T(8,128)(2,1)S(1)}, u32[]{:S(2)}, u32[]{:S(2)}) collective-permute-start(bf16[2,1,1,64,512]{4,3,1,0,2:T(8,128)(2,1)S(1)} %get-tuple-element.208), channel_id=1, source_target_pairs={{0,4},{1,5},{2,6},{3,7},{4,0},{5,1},{6,2},{7,3},{8,12},{9,13},{10,... | collective-permute-start | bytes 393224 | tf_op jit(solution)/shard_map/ppermute | solution.py:20
  336.0 25.3 %collective-permute-start.8 = (bf16[2,1,1,64,512]{4,3,1,0,2:T(8,128)(2,1)S(1)}, bf16[2,1,1,64,512]{4,3,1,0,2:T(8,128)(2,1)S(1)}, u32[]{:S(2)}, u32[]{:S(2)}) collective-permute-start(bf16[2,1,1,64,512]{4,3,1,0,2:T(8,128)(2,1)S(1)} %get-tuple-element.207), channel_id=1, source_target_pairs={{0,3},{1,4},{2,5},{3,6},{4,7},{5,0},{6,1},{7,2},{8,11},{9,12},{10,... | collective-permute-start | bytes 393224 | tf_op jit(solution)/shard_map/ppermute | solution.py:20
  344.1 17.8 %copy-start.7 = (bf16[2,8,1,64,512]{4,3,1,0,2:T(8,128)(2,1)}, bf16[2,8,1,64,512]{4,3,1,0,2:T(8,128)(2,1)S(1)}, u32[]{:S(2)}) copy-start(bf16[2,8,1,64,512]{4,3,1,0,2:T(8,128)(2,1)S(1)} %slice_dynamic-update-slice_fusion.1) | copy-start | bytes 3145732
  344.1 17.8 %collective-permute-start.9 = (bf16[2,1,1,64,512]{4,3,1,0,2:T(8,128)(2,1)S(1)}, bf16[2,1,1,64,512]{4,3,1,0,2:T(8,128)(2,1)S(1)}, u32[]{:S(2)}, u32[]{:S(2)}) collective-permute-start(bf16[2,1,1,64,512]{4,3,1,0,2:T(8,128)(2,1)S(1)} %get-tuple-element.206), channel_id=1, source_target_pairs={{0,2},{1,3},{2,4},{3,5},{4,6},{5,7},{6,0},{7,1},{8,10},{9,11},{10,... | collective-permute-start | bytes 393224 | tf_op jit(solution)/shard_map/ppermute | solution.py:20
  344.9 18.0 %collective-permute-start.10 = (bf16[2,1,1,64,512]{4,3,1,0,2:T(8,128)(2,1)S(1)}, bf16[2,1,1,64,512]{4,3,1,0,2:T(8,128)(2,1)S(1)}, u32[]{:S(2)}, u32[]{:S(2)}) collective-permute-start(bf16[2,1,1,64,512]{4,3,1,0,2:T(8,128)(2,1)S(1)} %get-tuple-element.205), channel_id=1, source_target_pairs={{0,1},{1,2},{2,3},{3,4},{4,5},{5,6},{6,7},{7,0},{8,9},{9,10},{10,1... | collective-permute-start | bytes 393224 | tf_op jit(solution)/shard_map/ppermute | solution.py:20
  365.3 15.9 %copy-start.20 = (pred[8]{0:T(512)(128)(4,1)S(1)}, pred[8]{0:T(512)(128)(4,1)}, u32[]{:S(2)}) copy-start(pred[8]{0:T(512)(128)(4,1)} %copy-done.19) | copy-start | bytes 28
  365.3 15.9 %copy-start.26 = (s32[8]{0:T(128)S(1)}, s32[8]{0:T(128)}, u32[]{:S(2)}) copy-start(s32[8]{0:T(128)} %copy-done.25) | copy-start | bytes 100
  385.5 31.4 %collective-permute-start.25 = (bf16[256,5120]{1,0:T(8,128)(2,1)S(1)}, bf16[256,5120]{1,0:T(8,128)(2,1)S(1)}, u32[]{:S(2)}, u32[]{:S(2)}) collective-permute-start(bf16[256,5120]{1,0:T(8,128)(2,1)S(1)} %pad_maximum_fusion), channel_id=1, source_target_pairs={{8,0},{16,8},{24,16},{0,24},{9,1},{17,9},{25,17},{1,25},{10,2},{18... | collective-permute-start | bytes 7864328 | tf_op jit(solution)/shard_map/ppermute | solution.py:46
  (24 other events, 160.3 us)
Sparse Core Ops, SparseCore 0:
  30.9 86.0 all-reduce.7
  277.5 97.8 all-reduce.5
